TPU v7x, 128 devices: a whole 4x4x4 slice. The times are simulated.
128 devices in a mesh: dp: 8 (over x, y_lo), expert: 16 (over z, y_hi, core).
Axes of the slice: x: 4, y: 4 (y_hi: 2, y_lo: 2; y = y_hi * 2 + y_lo), z: 4, core: 2. Of those that a mesh axis runs over, the one named last changes fastest.
Arguments:
- tokens: bfloat16 [16384, 3072], P(('dp', 'expert')), parts along dimension 0, may hold values from -6 to 6
- expert_ids: int32 [16384, 4], P(('dp', 'expert')), parts along dimension 0, may hold values from 0 to 15, as said below
- gate_weights: float32 [16384, 4], P(('dp', 'expert')), parts along dimension 0, may hold values from 0.05 to 0.5
- slot_rows: int32 [128, 16, 64], P(('dp', 'expert')), parts along dimension 0, may hold values from 0 to 128, as said below
- w_in: bfloat16 [16, 3072, 2560], P('expert'), may hold values from -0.109375 to 0.109375
- w_out: bfloat16 [16, 1280, 3072], P('expert'), may hold values from -0.15625 to 0.15625
Outputs:
- mixed: bfloat16 [16384, 3072], P(('dp', 'expert')), parts along dimension 0
There are 8 independent parts, one for each index of `dp`. A program takes and returns all parts, laid end to end along the dimension named above; an argument that names none is the same for every part. Nothing has to cross between parts.
Inputs may be any that keep to these rules, and one draw needn't show every extreme that they name: `expert_ids`: each row names 4 different experts. slot_rows[s, e] lists, in increasing order, the rows of shard s whose tokens name expert e, the first 64 of them, then 128 in the remaining slots; in every draw some expert has all 64 slots filled by every shard.
All inputs are finite; a program needn't handle non-finite values.
Results may differ from a plain program's by a relative error of at most 0.0063.
Values may be sent and summed in bfloat16 or wider, within the bound.
No kernel may reach another device: no remote copies, remote signals or barrier semaphores. Data moves between devices by JAX's collectives and lax.ppermute only.
A program may use at most 128 MiB of HBM per device.

v0:
```python
import jax
import jax.numpy as jnp
from jax import lax
from jax.sharding import PartitionSpec as P


def expert_block(rows_in, w_first, w_second):
    features = rows_in.shape[-1]
    hidden_units = w_second.shape[0]
    flat = rows_in.reshape(-1, features)
    projected = jnp.dot(flat, w_first, preferred_element_type=jnp.float32)
    intermediate_activation = (
        jax.nn.silu(projected[:, :hidden_units]) * projected[:, hidden_units:]
    ).astype(jnp.bfloat16)
    result = jnp.dot(intermediate_activation, w_second, preferred_element_type=jnp.float32).astype(
        jnp.bfloat16
    )
    return result.reshape(rows_in.shape)


def shards(tokens, expert_ids, gate_weights, slot_rows, w_in, w_out):
    tok_rows, features = tokens.shape
    experts = slot_rows.shape[1]
    capacity = slot_rows.shape[2]
    w_first = w_in[0]
    w_second = w_out[0]
    own_rows = slot_rows[0]
    occupied = own_rows < tok_rows
    clipped = jnp.minimum(own_rows, tok_rows - 1)
    matches = (
        expert_ids[:, :, None] == jnp.arange(experts, dtype=jnp.int32)[None, None, :]
    ).astype(jnp.float32)
    gate_of = jnp.einsum("tk,tke->et", gate_weights, matches)
    slot_gate = jnp.where(occupied, jnp.take_along_axis(gate_of, clipped, axis=1), 0.0).astype(
        jnp.bfloat16
    )
    this_device = lax.axis_index("expert")
    gathered, all_lists = (
        lax.all_gather(tokens, "expert", axis=0, tiled=True),
        lax.all_gather(slot_rows, "expert", axis=0, tiled=True),
    )
    own_lists = lax.dynamic_index_in_dim(all_lists, this_device, axis=1, keepdims=False)
    offsets = jnp.arange(experts, dtype=jnp.int32)[:, None] * tok_rows
    positions = jnp.where(own_lists < tok_rows, own_lists + offsets, gathered.shape[0])
    selected = jnp.take(gathered, positions.reshape(-1), axis=0, mode="fill", fill_value=0)
    layer_response = expert_block(selected.reshape(experts, capacity, features), w_first, w_second)
    returned = lax.all_to_all(layer_response, "expert", split_axis=0, concat_axis=0, tiled=True)
    expert_onehot = own_rows.reshape(-1)[None, :] == jnp.arange(tok_rows, dtype=jnp.int32)[:, None]
    mixing = jnp.where(expert_onehot, slot_gate.reshape(-1)[None, :], jnp.zeros((), jnp.bfloat16))
    summed = jnp.dot(mixing, returned.reshape(-1, features), preferred_element_type=jnp.float32)
    return summed.astype(jnp.bfloat16)


def solution(mesh):
    in_specs = (
        P(("dp", "expert"), None),
        P(("dp", "expert"), None),
        P(("dp", "expert"), None),
        P(("dp", "expert"), None, None),
        P("expert", None, None),
        P("expert", None, None),
    )
    out_specs = P(("dp", "expert"), None)
    return jax.shard_map(shards, mesh=mesh, in_specs=in_specs, out_specs=out_specs, check_vma=False)
```

profile of v0, /device:TPU:1, one launch (start us, length us, event | category | flops | bytes accessed | tf_op | source)
XLA Modules:
  0.0 244.3 jit_solution(8252859320478719966)
XLA Ops:
  6.5 0.7 all-gather.2.cloned.1.call-update
  7.3 0.1 add.75
  7.3 0.1 add.79
  7.4 0.1 add.76
  7.5 28.1 %all_gather.6 = s32[16,16,64]{2,1,0:T(8,128)S(1)} all-gather(s32[1,16,64]{2,1,0:T(8,128)} %param.9), channel_id=1, replica_groups=mesh['dp'=8,'expert'=16] {'expert'}, dimensions={0}, use_global_device_ids=true | all-gather | bytes 69632 | tf_op jit(solution)/shard_map/all_gather | solution.py:40
  35.6 0.5 broadcast.165
  36.1 0.7 fusion.26
  36.8 0.1 squeeze.13
  36.9 0.1 squeeze.14
  37.0 67.5 %all-gather.2.cloned.1.call-done = bf16[2048,3072]{1,0:T(8,128)(2,1)} async-done(((bf16[128,3072]{1,0:T(8,128)(2,1)}), bf16[2048,3072]{1,0:T(8,128)(2,1)}) %all-gather.2.cloned.1.call-update) | async-done | bytes 12582928 | tf_op jit(solution)/shard_map/all_gather | solution.py:39
  104.5 18.4 %gather_fusion = bf16[1024,3072]{1,0:T(8,128)(2,1)} fusion(bf16[2048,3072]{1,0:T(8,128)(2,1)} %all-gather.2.cloned.1.call-done, s32[1024]{0:T(1024)S(1)} %broadcast_clamp_fusion), kind=kCustom, calls=%fused_computation | custom fusion | bytes 12587008 | tf_op jit(solution)/shard_map/jit(_take)/gather | solution.py:45
  122.9 21.2 %fusion = f32[1024,2560]{1,0:T(8,128)S(1)} fusion(bf16[1,3072,2560]{2,1,0:T(8,128)(2,1)} %param.10, bf16[1024,3072]{1,0:T(8,128)(2,1)} %gather_fusion, pred[1024]{0:T(1024)(128)(4,1)S(1)} %compare_and_fusion), kind=kOutput, calls=%fused_computation.2 | convolution fusion | flops 16109273088 | bytes 32506880 | tf_op jit(solution)/shard_map/dot_general | solution.py:11
  144.1 0.0 copy-done.3
  144.1 10.3 %fusion.6 = bf16[1024,3072]{1,0:T(8,128)(2,1)} fusion(bf16[1,1280,3072]{2,1,0:T(8,128)(2,1)S(1)} %copy-done.3, f32[1024,2560]{1,0:T(8,128)S(1)} %fusion), kind=kOutput, calls=%fused_computation.8 | convolution fusion | flops 8064073728 | bytes 24641536 | tf_op jit(solution)/shard_map/dot_general | solution.py:15
  154.4 4.7 %all-to-all-start = ((bf16[16,64,3072]{2,1,0:T(8,128)(2,1)}), bf16[16,64,3072]{2,1,0:T(8,128)(2,1)}, u32[]{:S(2)}, u32[]{:S(2)}) async-start(bf16[16,64,3072]{2,1,0:T(8,128)(2,1)} %bitcast.24), calls=%async_computation | async-start | bytes 12582912 | tf_op jit(solution)/shard_map/all_to_all | solution.py:47
  159.1 0.1 eq.28
  159.2 0.1 reshape.124
  159.3 0.0 copy-done.1
  159.3 0.1 copy.9
  159.4 0.2 copy.10
  159.6 0.4 fusion.16
  159.9 7.3 %gather_fusion.1 = bf16[1024]{0:T(1024)(128)(2,1)S(1)} fusion(f32[16,128]{0,1:T(8,128)S(1)} %bitcast.23, s32[1024]{0:T(1024)S(1)} %reshape.124), kind=kCustom, calls=%fused_computation.1 | custom fusion | bytes 12288 | tf_op jit(solution)/shard_map/jit(take_along_axis)/gather | solution.py:34
  167.2 65.6 %all-to-all-done = bf16[16,64,3072]{2,1,0:T(8,128)(2,1)} async-done(((bf16[16,64,3072]{2,1,0:T(8,128)(2,1)}), bf16[16,64,3072]{2,1,0:T(8,128)(2,1)}, u32[]{:S(2)}, u32[]{:S(2)}) %all-to-all-start) | async-done | bytes 6291488 | tf_op jit(solution)/shard_map/all_to_all | solution.py:47
  232.8 4.7 %convolution_convert_fusion = bf16[128,3072]{1,0:T(8,128)(2,1)} fusion(bf16[1024,3072]{1,0:T(8,128)(2,1)} %bitcast.9, s32[1024]{0:T(1024)S(1)} %eq.28, bf16[1024]{0:T(1024)(128)(2,1)S(1)} %select_convert_fusion), kind=kOutput, calls=%fused_computation.11 | convolution fusion | flops 805961728 | bytes 7084032 | tf_op jit(solution)/shard_map/dot_general | solution.py:50
  (13 shorter events, 0.1 us)
Async XLA Ops:
  6.5 98.0 %all-gather.2.cloned.1.call-start = ((), (), s32[]{:S(2)}) async-start(), calls=%async_computation.1 | async-start | bytes 13369344 | tf_op jit(solution)/shard_map/all_gather | solution.py:39
  122.9 21.2 %copy-start.3 = (bf16[1,1280,3072]{2,1,0:T(8,128)(2,1)S(1)}, bf16[1,1280,3072]{2,1,0:T(8,128)(2,1)}, u32[]{:S(2)}) copy-start(bf16[1,1280,3072]{2,1,0:T(8,128)(2,1)} %param.11) | copy-start | bytes 23592964
  154.4 4.7 %copy-start = (s32[1,16,64]{2,1,0:T(8,128)S(1)}, s32[1,16,64]{2,1,0:T(8,128)}, u32[]{:S(2)}) copy-start(s32[1,16,64]{2,1,0:T(8,128)} %param.9) | copy-start | bytes 12292
  154.4 4.9 %copy-start.1 = (s32[128,4]{0,1:T(4,128)S(1)}, s32[128,4]{0,1:T(4,128)}, u32[]{:S(2)}) copy-start(s32[128,4]{0,1:T(4,128)} %param.7) | copy-start | bytes 6148
  154.4 5.0 %copy-start.2 = (f32[128,4]{0,1:T(4,128)S(1)}, f32[128,4]{0,1:T(4,128)}, u32[]{:S(2)}) copy-start(f32[128,4]{0,1:T(4,128)} %param.8) | copy-start | bytes 6148
  154.4 78.4 %all-to-all-start = ((bf16[16,64,3072]{2,1,0:T(8,128)(2,1)}), bf16[16,64,3072]{2,1,0:T(8,128)(2,1)}, u32[]{:S(2)}, u32[]{:S(2)}) async-start(bf16[16,64,3072]{2,1,0:T(8,128)(2,1)} %bitcast.24), calls=%async_computation | async-start | bytes 12582912 | tf_op jit(solution)/shard_map/all_to_all | solution.py:47
Sparse Core Ops, SparseCore 0:
  9.8 94.6 all-gather.1
where the time goes:
time: 245 us; the launch traced here: 244 us
  waiting for transfers between devices  134 us (55%)
  matrix products  36.5 us (15%)
  blocking collectives  28.1 us (11%)
  local copies, waits for them, and re-layouts  27.6 us (11%)
  between operations  13.5 us (6%)
  starting transfers between devices  4.74 us (2%)
    all_gather x1, waiting for transfers between devices, shards(): lax.all_gather(tokens, 'expert', axis=0, tiled=True)  67.5 us
    all_to_all x1, waiting for transfers between devices, shards(): lax.all_to_all(layer_response, 'expert', split_axis=0, concat_axis=0, til...  65.6 us
    all_gather x1, blocking collectives, shards(): lax.all_gather(slot_rows, 'expert', axis=0, tiled=True)  28.1 us
    dot_general x1, matrix products, expert_block(): projected = jnp.dot(flat, w_first, preferred_element_type=jnp.float32)  21.2 us
    gather x1, local copies, waits for them, and re-layouts, shards(): jnp.take(gathered, positions.reshape(-1), axis=0, mode='fill', fill_value=0)  18.4 us
    dot_general x1, matrix products, expert_block(): jnp.dot(intermediate_activation, w_second, preferred_element_type=jnp.flo...  10.3 us
    gather x2, local copies, waits for them, and re-layouts, shards(): jnp.take_along_axis(gate_of, clipped, axis=1)  7.32 us
  transfers between devices with their start and end apart: 2, of which 2 were waited for; matrix products, arithmetic and copies ran while one was open for 4% of the time, Pallas kernels for 0%

commit v1 on v0

--- a/solution.py
+++ b/solution.py
@@ -35,8 +35,17 @@
         jnp.bfloat16
     )
     this_device = lax.axis_index("expert")
+    links_launch = lambda z, link_axis: jnp.concatenate(
+        lax.all_to_all(
+            jnp.stack([z] * lax.axis_size(link_axis), axis=0),
+            axis_name=link_axis,
+            split_axis=0,
+            concat_axis=0,
+        ),
+        axis=0,
+    )
     gathered, all_lists = (
-        lax.all_gather(tokens, "expert", axis=0, tiled=True),
+        links_launch(tokens, "expert"),
         lax.all_gather(slot_rows, "expert", axis=0, tiled=True),
     )
     own_lists = lax.dynamic_index_in_dim(all_lists, this_device, axis=1, keepdims=False)

time: 245 us -> 310 us (1.27)
  blocking collectives: 28.1 us -> 155 us
  waiting for transfers between devices: 134 us -> 65.6 us
  between operations: 13.5 us -> 0.1 us
  starting transfers between devices: 4.74 us -> 14.3 us
  local copies, waits for them, and re-layouts: 27.6 us -> 34.8 us
  matrix products: 36.5 us -> 39.8 us
    all_gather x1, blocking collectives: 28.1 us -> 155 us  [shards(): lax.all_gather(slot_rows, 'expert', axis=0, tiled=True)]
    all_gather x1 -> x0, waiting for transfers between devices: 67.5 us -> none  [shards(): lax.all_gather(tokens, 'expert', axis=0, tiled=True)]
    all_to_all x0 -> x1, starting transfers between devices: none -> 9.59 us  [shards(): lax.all_to_all(jnp.stack([z] * lax.axis_size(link_axis), axis=0), axis_na...]
    another operation x0 -> x1, local copies, waits for them, and re-layouts: none -> 7.21 us  [shards(): jnp.stack([z] * lax.axis_size(link_axis), axis=0)]
    dot_general x1, matrix products: 10.3 us -> 13.7 us  [expert_block(): jnp.dot(intermediate_activation, w_second, preferred_element_type=jnp.flo...]
  transfers between devices with their start and end apart: 2 -> 2, of which waited for: 2 -> 1; matrix products, arithmetic and copies ran while one was open for 4% -> 3% of each run, Pallas kernels for 0% -> 0%
where the time goes in v1:
time: 310 us; the launch traced here: 309 us
  blocking collectives  155 us (50%)
  waiting for transfers between devices  65.6 us (21%)
  matrix products  39.8 us (13%)
  local copies, waits for them, and re-layouts  34.8 us (11%)
  starting transfers between devices  14.3 us (5%)
    all_gather x1, blocking collectives, shards(): lax.all_gather(slot_rows, 'expert', axis=0, tiled=True)  155 us
    all_to_all x1, waiting for transfers between devices, shards(): lax.all_to_all(layer_response, 'expert', split_axis=0, concat_axis=0, til...  65.6 us
    dot_general x1, matrix products, expert_block(): projected = jnp.dot(flat, w_first, preferred_element_type=jnp.float32)  21.1 us
    gather x1, local copies, waits for them, and re-layouts, shards(): jnp.take(gathered, positions.reshape(-1), axis=0, mode='fill', fill_value=0)  18.4 us
    dot_general x1, matrix products, expert_block(): jnp.dot(intermediate_activation, w_second, preferred_element_type=jnp.flo...  13.7 us
    all_to_all x1, starting transfers between devices, shards(): lax.all_to_all(jnp.stack([z] * lax.axis_size(link_axis), axis=0), axis_na...  9.59 us
    gather x2, local copies, waits for them, and re-layouts, shards(): jnp.take_along_axis(gate_of, clipped, axis=1)  7.32 us
    another operation x1, local copies, waits for them, and re-layouts, shards(): jnp.stack([z] * lax.axis_size(link_axis), axis=0)  7.21 us
  transfers between devices with their start and end apart: 2, of which 1 were waited for; matrix products, arithmetic and copies ran while one was open for 3% of the time, Pallas kernels for 0%

profile of v1, /device:TPU:1, one launch (start us, length us, event | category | flops | bytes accessed | tf_op | source)
XLA Modules:
  0.0 309.4 jit_solution(4084966006928889066)
XLA Ops:
  0.0 7.2 %stack.2 = bf16[16,128,3072]{2,1,0:T(8,128)(2,1)} broadcast(bf16[128,3072]{1,0:T(8,128)(2,1)} %param.6), dimensions={1,2} | broadcast | bytes 13369344 | tf_op jit(solution)/shard_map/stack | solution.py:40
  7.2 9.6 %all-to-all-start = ((bf16[16,128,3072]{2,1,0:T(8,128)(2,1)}), bf16[16,128,3072]{2,1,0:T(8,128)(2,1)}, u32[]{:S(2)}, u32[]{:S(2)}) async-start(bf16[16,128,3072]{2,1,0:T(8,128)(2,1)} %stack.2), calls=%async_computation | async-start | bytes 25165824 | tf_op jit(solution)/shard_map/all_to_all | solution.py:39
  16.8 0.1 add.75
  16.9 0.1 add.79
  17.0 0.1 add.76
  17.0 0.0 copy-done
  17.0 154.8 %all_gather.3 = s32[16,16,64]{2,1,0:T(8,128)S(1)} all-gather(s32[1,16,64]{2,1,0:T(8,128)S(1)} %copy-done), channel_id=1, replica_groups=mesh['dp'=8,'expert'=16] {'expert'}, dimensions={0}, use_global_device_ids=true | all-gather | bytes 69632 | tf_op jit(solution)/shard_map/all_gather | solution.py:49
  171.9 0.5 broadcast.167
  172.4 0.7 fusion.26
  173.1 0.1 squeeze.14
  173.1 0.1 squeeze.13
  173.3 0.0 all-to-all-done
  173.3 18.4 %gather_fusion = bf16[1024,3072]{1,0:T(8,128)(2,1)} fusion(bf16[2048,3072]{1,0:T(8,128)(2,1)} %bitcast.5, s32[1024]{0:T(1024)S(1)} %broadcast_clamp_fusion), kind=kCustom, calls=%fused_computation | custom fusion | bytes 12587008 | tf_op jit(solution)/shard_map/jit(_take)/gather | solution.py:54
  191.7 21.1 %fusion = f32[1024,2560]{1,0:T(8,128)S(1)} fusion(bf16[1,3072,2560]{2,1,0:T(8,128)(2,1)} %param.10, bf16[1024,3072]{1,0:T(8,128)(2,1)} %gather_fusion, pred[1024]{0:T(1024)(128)(4,1)S(1)} %compare_and_fusion), kind=kOutput, calls=%fused_computation.2 | convolution fusion | flops 16109273088 | bytes 32506880 | tf_op jit(solution)/shard_map/dot_general | solution.py:11
  212.7 13.7 %fusion.6 = bf16[1024,3072]{1,0:T(8,128)(2,1)} fusion(bf16[1,1280,3072]{2,1,0:T(8,128)(2,1)} %param.11, f32[1024,2560]{1,0:T(8,128)S(1)} %fusion), kind=kOutput, calls=%fused_computation.8 | convolution fusion | flops 8064073728 | bytes 24641536 | tf_op jit(solution)/shard_map/dot_general | solution.py:15
  226.5 4.7 %all-to-all-start.1 = ((bf16[16,64,3072]{2,1,0:T(8,128)(2,1)}), bf16[16,64,3072]{2,1,0:T(8,128)(2,1)}, u32[]{:S(2)}, u32[]{:S(2)}) async-start(bf16[16,64,3072]{2,1,0:T(8,128)(2,1)} %bitcast.25), calls=%async_computation.1 | async-start | bytes 12582912 | tf_op jit(solution)/shard_map/all_to_all | solution.py:56
  231.1 0.1 eq.28
  231.2 0.2 copy.10
  231.4 0.1 copy.9
  231.5 0.1 reshape.130
  231.6 0.3 fusion.16
  231.9 7.3 %gather_fusion.1 = bf16[1024]{0:T(1024)(128)(2,1)S(1)} fusion(f32[16,128]{0,1:T(8,128)S(1)} %bitcast.24, s32[1024]{0:T(1024)S(1)} %reshape.130), kind=kCustom, calls=%fused_computation.1 | custom fusion | bytes 12288 | tf_op jit(solution)/shard_map/jit(take_along_axis)/gather | solution.py:34
  239.2 65.6 %all-to-all-done.1 = bf16[16,64,3072]{2,1,0:T(8,128)(2,1)} async-done(((bf16[16,64,3072]{2,1,0:T(8,128)(2,1)}), bf16[16,64,3072]{2,1,0:T(8,128)(2,1)}, u32[]{:S(2)}, u32[]{:S(2)}) %all-to-all-start.1) | async-done | bytes 6291488 | tf_op jit(solution)/shard_map/all_to_all | solution.py:56
  304.8 4.7 %convolution_convert_fusion = bf16[128,3072]{1,0:T(8,128)(2,1)} fusion(bf16[1024,3072]{1,0:T(8,128)(2,1)} %bitcast.10, s32[1024]{0:T(1024)S(1)} %eq.28, bf16[1024]{0:T(1024)(128)(2,1)S(1)} %select_convert_fusion), kind=kOutput, calls=%fused_computation.11 | convolution fusion | flops 805961728 | bytes 7084032 | tf_op jit(solution)/shard_map/dot_general | solution.py:59
  (11 shorter events, 0.1 us)
Async XLA Ops:
  7.2 9.8 %copy-start = (s32[1,16,64]{2,1,0:T(8,128)S(1)}, s32[1,16,64]{2,1,0:T(8,128)}, u32[]{:S(2)}) copy-start(s32[1,16,64]{2,1,0:T(8,128)} %param.9) | copy-start | bytes 12292
  7.2 166.1 %all-to-all-start = ((bf16[16,128,3072]{2,1,0:T(8,128)(2,1)}), bf16[16,128,3072]{2,1,0:T(8,128)(2,1)}, u32[]{:S(2)}, u32[]{:S(2)}) async-start(bf16[16,128,3072]{2,1,0:T(8,128)(2,1)} %stack.2), calls=%async_computation | async-start | bytes 25165824 | tf_op jit(solution)/shard_map/all_to_all | solution.py:39
  226.5 4.8 %copy-start.1 = (f32[128,4]{0,1:T(4,128)S(1)}, f32[128,4]{0,1:T(4,128)}, u32[]{:S(2)}) copy-start(f32[128,4]{0,1:T(4,128)} %param.8) | copy-start | bytes 6148
  226.5 4.9 %copy-start.2 = (s32[128,4]{0,1:T(4,128)S(1)}, s32[128,4]{0,1:T(4,128)}, u32[]{:S(2)}) copy-start(s32[128,4]{0,1:T(4,128)} %param.7) | copy-start | bytes 6148
  226.5 78.3 %all-to-all-start.1 = ((bf16[16,64,3072]{2,1,0:T(8,128)(2,1)}), bf16[16,64,3072]{2,1,0:T(8,128)(2,1)}, u32[]{:S(2)}, u32[]{:S(2)}) async-start(bf16[16,64,3072]{2,1,0:T(8,128)(2,1)} %bitcast.25), calls=%async_computation.1 | async-start | bytes 12582912 | tf_op jit(solution)/shard_map/all_to_all | solution.py:56
